TPU v7x, 256 devices: a whole 4x4x8 slice. The times are simulated.
256 devices in a mesh: seq: 32 (over x, z), tp: 8 (over y, core).
Axes of the slice: x: 4, y: 4, z: 8, core: 2. Of those that a mesh axis runs over, the one named last changes fastest.
Arguments:
- tokens: bfloat16 [32768, 2048], P('seq', 'tp'), may hold values from -6 to 6
- w_inner: bfloat16 [2048, 2, 4096], P('seq', None, 'tp'), may hold values from -0.125 to 0.125
- w_states: bfloat16 [2048, 256], P('seq'), may hold values from -0.125 to 0.125
- w_step: bfloat16 [2048, 64], P('seq', 'tp'), may hold values from -0.125 to 0.125
- conv_inner: float32 [4, 4096], P(None, 'tp'), may hold values from -3 to 3
- conv_states: float32 [4, 256], replicated, may hold values from -3 to 3
- decay_rate: float32 [64], P('tp'), may hold values from 0 to 1, as said below
- step_bias: float32 [64], P('tp'), may hold values from -1 to 0.5
- skip_gain: float32 [64], P('tp'), may hold values from 0.5 to 1.5
- norm_gain: float32 [4096], P('tp'), may hold values from 0.5 to 1.5
- w_output: bfloat16 [4096, 2048], P('tp', 'seq'), may hold values from -0.09375 to 0.09375
- block_owner: int32 [128], replicated, may hold values from 0 to 19, as said below
- lengths: int32 [20], replicated, may hold values from 1 to 16384, as said below
Outputs:
- mixed: bfloat16 [32768, 2048], P('seq', 'tp')
Inputs may be any that keep to these rules, and one draw needn't show every extreme that they name: `block_owner`: each prompt's blocks are consecutive, prompt r has ceil(lengths[r] / 256) of them, and the prompts follow one another in an order drawn afresh; one prompt has 64 blocks and is neither the first nor the last in that order. `lengths`: one prompt has exactly 16384 tokens. `decay_rate`: Positive.
All inputs are finite; a program needn't handle non-finite values.
Results may differ from a plain program's by a relative error of at most 0.0075.
Values may be sent and summed in bfloat16 or wider, within the bound.
No kernel may reach another device: no remote copies, remote signals or barrier semaphores. Data moves between devices by JAX's collectives and lax.ppermute only.
A program may use at most 64 MiB of HBM per device.

v0:
```python
import jax
import jax.numpy as jnp
from jax import lax
from jax.sharding import PartitionSpec as P

BLOCK = 256


def passed_along(value, axis, by):
    count = lax.axis_size(axis)
    pairs = [(i, i + by) for i in range(count) if 0 <= i + by < count]
    return lax.ppermute(value, axis, pairs)


def convolve(values, edge_rows, weights, in_block, carry_on):
    lag_rows = weights.shape[0] - 1
    row_total = values.shape[0]
    widened = jnp.concatenate([edge_rows, values], axis=0).astype(jnp.float32)
    total = jnp.zeros(values.shape, jnp.float32)
    for offset in range(weights.shape[0]):
        shifted = widened[lag_rows - offset : lag_rows - offset + row_total]
        keeping = (in_block >= offset) | carry_on
        total = total + jnp.where(keeping[:, None], shifted, 0.0) * weights[offset]
    return jax.nn.silu(total).astype(jnp.bfloat16)


def on_device(
    tokens,
    w_inner,
    w_states,
    w_step,
    conv_inner,
    conv_states,
    decay_rate,
    step_bias,
    skip_gain,
    norm_gain,
    w_output,
    block_owner,
    lengths,
):
    row_count = tokens.shape[0]
    local_blocks = row_count // BLOCK
    total_blocks = block_owner.shape[0]
    heads_here = w_step.shape[1]
    inner_here = w_inner.shape[2]
    state_size = w_states.shape[1] // 2
    head_size = inner_here // heads_here
    lag_rows = conv_inner.shape[0] - 1
    block_ids = jnp.arange(total_blocks, dtype=jnp.int32)
    same_owner = block_owner[:, None] == block_owner[None, :]
    first_block = jnp.min(jnp.where(same_owner, block_ids[None, :], total_blocks), axis=1)
    starting = (first_block == block_ids).astype(jnp.int32)
    request_ids = jnp.arange(lengths.shape[0], dtype=jnp.int32)
    own_length = jnp.sum(
        jnp.where(block_owner[:, None] == request_ids[None, :], lengths[None, :], 0), axis=1
    )
    valid_rows = jnp.clip(own_length - (block_ids - first_block) * BLOCK, 0, BLOCK)
    seq_index = lax.axis_index("seq")
    local_start = lax.dynamic_slice_in_dim(starting, seq_index * local_blocks, local_blocks)
    local_valid = lax.dynamic_slice_in_dim(valid_rows, seq_index * local_blocks, local_blocks)
    in_block = jnp.arange(row_count, dtype=jnp.int32) % BLOCK
    carry_on = jnp.repeat(local_start == 0, BLOCK)
    whole = lax.all_gather(tokens, "tp", axis=1, tiled=True)
    pieces = (
        lax.all_gather(w_inner, "seq", axis=0, tiled=True),
        lax.all_gather(w_states, "seq", axis=0, tiled=True),
        lax.all_gather(w_step, "seq", axis=0, tiled=True),
    )
    count = pieces[0].shape[0]
    inner_sum = jnp.dot(
        whole, pieces[0].reshape(count, 2 * inner_here), preferred_element_type=jnp.float32
    )
    states_sum = jnp.dot(whole, pieces[1], preferred_element_type=jnp.float32)
    step_sum = jnp.dot(whole, pieces[2], preferred_element_type=jnp.float32)
    projected = inner_sum.astype(jnp.bfloat16)
    gate_in = projected[:, :inner_here]
    x_in = projected[:, inner_here:]
    bc_in = states_sum.astype(jnp.bfloat16)
    step_raw = step_sum.astype(jnp.bfloat16)
    edge_inner, edge_states = passed_along(
        (x_in[row_count - lag_rows :], bc_in[row_count - lag_rows :]), "seq", 1
    )
    x_conv = convolve(x_in, edge_inner, conv_inner, in_block, carry_on)
    bc_conv = convolve(bc_in, edge_states, conv_states, in_block, carry_on)
    step_size = jax.nn.softplus(step_raw.astype(jnp.float32) + step_bias)
    log_decay = -decay_rate * step_size
    x_heads = x_conv.reshape(local_blocks, BLOCK, heads_here, head_size)
    b_rows = bc_conv[:, :state_size].reshape(local_blocks, BLOCK, state_size)
    c_rows = bc_conv[:, state_size:].reshape(local_blocks, BLOCK, state_size)
    step_blocks = step_size.reshape(local_blocks, BLOCK, heads_here)
    cumulative = jnp.cumsum(log_decay.reshape(local_blocks, BLOCK, heads_here), axis=1)
    causal = jnp.arange(BLOCK)[:, None] >= jnp.arange(BLOCK)[None, :]
    spread = cumulative[:, :, None, :] - cumulative[:, None, :, :]
    decays = jnp.exp(jnp.where(causal[None, :, :, None], spread, -jnp.inf))
    intersection = jnp.einsum("cin,cjn->cij", c_rows, b_rows, preferred_element_type=jnp.float32)
    mixing = (decays * intersection[:, :, :, None] * step_blocks[:, None, :, :]).astype(
        jnp.bfloat16
    )
    y_inner = jnp.einsum("cijh,cjhp->cihp", mixing, x_heads, preferred_element_type=jnp.float32)
    final_log = cumulative[:, -1, :]
    tail_weight = jnp.exp(final_log[:, None, :] - cumulative) * step_blocks
    weighted_b = (tail_weight[:, :, :, None] * b_rows.astype(jnp.float32)[:, :, None, :]).astype(
        jnp.bfloat16
    )
    fresh = jnp.einsum("cjhn,cjhp->chnp", weighted_b, x_heads, preferred_element_type=jnp.float32)
    keep_flag = jnp.where(local_start == 1, 0.0, 1.0).astype(jnp.float32)
    block_gain_each = jnp.exp(final_log) * keep_flag[:, None]

    def fold_block(carry, item):
        gain_now, fresh_now = item
        return ((carry[0] * gain_now, gain_now[:, None, None] * carry[1] + fresh_now), None)

    zero_state = jnp.zeros((heads_here, state_size, head_size), jnp.float32)
    unit_gain = jnp.ones((heads_here,), jnp.float32)
    (block_gain, block_state), _ = lax.scan(
        fold_block, (unit_gain, zero_state), (block_gain_each, fresh)
    )

    def relay(iteration, entering_now):
        return passed_along(block_gain[:, None, None] * entering_now + block_state, "seq", 1)

    entering = lax.fori_loop(0, lax.axis_size("seq") - 1, relay, zero_state)

    def pass_block(previous, item):
        log_now, keep_now, fresh_now = item
        incoming = previous * keep_now
        return (jnp.exp(log_now)[:, None, None] * incoming + fresh_now, incoming)

    _, incoming_all = lax.scan(pass_block, entering, (final_log, keep_flag, fresh))
    incoming_half = incoming_all.astype(jnp.bfloat16)
    y_carry = jnp.exp(cumulative)[:, :, :, None] * jnp.einsum(
        "cin,chnp->cihp", c_rows, incoming_half, preferred_element_type=jnp.float32
    )
    y_total = (y_inner + y_carry).reshape(row_count, inner_here) + jnp.repeat(skip_gain, head_size)[
        None, :
    ] * x_conv.astype(jnp.float32)
    gated = y_total * jax.nn.silu(gate_in.astype(jnp.float32))
    squares = lax.psum(jnp.sum(gated * gated, axis=1), "tp")
    square_mean = squares / (inner_here * lax.axis_size("tp"))
    normed = (gated * lax.rsqrt(square_mean + 1e-05)[:, None] * norm_gain).astype(jnp.bfloat16)
    partial_out = jnp.dot(
        normed,
        lax.all_gather(w_output, "seq", axis=1, tiled=True),
        preferred_element_type=jnp.float32,
    )
    summed = lax.psum_scatter(partial_out, "tp", scatter_dimension=1, tiled=True)
    live = in_block < jnp.repeat(local_valid, BLOCK)
    return jnp.where(live[:, None], summed, 0.0).astype(jnp.bfloat16)


def solution(mesh):
    return jax.shard_map(
        on_device,
        mesh=mesh,
        in_specs=(
            P("seq", "tp"),
            P("seq", None, "tp"),
            P("seq", None),
            P("seq", "tp"),
            P(None, "tp"),
            P(),
            P("tp"),
            P("tp"),
            P("tp"),
            P("tp"),
            P("tp", "seq"),
            P(),
            P(),
        ),
        out_specs=P("seq", "tp"),
        check_vma=False,
    )
```

profile of v0, /device:TPU:1, one launch (start us, length us, event | category | flops | bytes accessed | tf_op | source)
XLA Modules:
  0.0 875.8 jit_solution(9368195072958447139)
XLA Ops:
  13.4 41.9 %all-gather = bf16[32,64,8]{1,2,0:T(8,128)(2,1)S(1)} all-gather(bf16[1,64,8]{1,2,0:T(8,128)(2,1)} %bitcast.99), channel_id=1, replica_groups=mesh['seq'=32,'tp'=8] {'seq'}, dimensions={0}, use_global_device_ids=true | all-gather | bytes 33792 | tf_op jit(solution)/shard_map/all_gather | solution.py:68
  57.5 27.5 %all-gather.10.cloned.1.call-done = bf16[2048,256]{1,0:T(8,128)(2,1)} async-done(((bf16[64,256]{1,0:T(8,128)(2,1)}), bf16[2048,256]{1,0:T(8,128)(2,1)}) %all-gather.10.cloned.1.call-update) | async-done | bytes 1048592 | tf_op jit(solution)/shard_map/all_gather | solution.py:67
  85.0 42.9 %all-gather.6.cloned.1.call-done = bf16[1024,2048]{1,0:T(8,128)(2,1)} async-done(((bf16[1024,256]{1,0:T(8,128)(2,1)}), bf16[1024,2048]{1,0:T(8,128)(2,1)}) %all-gather.6.cloned.1.call-update) | async-done | bytes 4194320 | tf_op jit(solution)/shard_map/all_gather | solution.py:64
  141.9 67.3 %all-gather.8.cloned.1.call-done = bf16[2048,2,512]{2,1,0:T(2,128)(2,1)} async-done(((bf16[64,2,512]{2,1,0:T(2,128)(2,1)}), bf16[2048,2,512]{2,1,0:T(2,128)(2,1)}) %all-gather.8.cloned.1.call-update) | async-done | bytes 4194320 | tf_op jit(solution)/shard_map/all_gather | solution.py:66
  245.5 454.9 %while.35 = (s32[]{:T(128)}, f32[8,128,64]{2,1,0:T(8,128)S(1)}, f32[8]{0:T(128)S(1)}, f32[8,128,64]{2,1,0:T(8,128)S(1)}, s32[]{:T(128)}) while((s32[]{:T(128)}, f32[8,128,64]{2,1,0:T(8,128)S(1)}, f32[8]{0:T(128)S(1)}, f32[8,128,64]{2,1,0:T(8,128)S(1)}, s32[]{:T(128)}) %tuple.77), condition=%wide.region_7.8_spmd, body=%wide.region_6.7_spmd.sunk | while | flops 131074 | bytes 1835141 | solution.py:123
  249.8 7.4 collective-permute-done
  262.2 9.9 %collective-permute-done = f32[8,128,64]{2,1,0:T(8,128)S(1)} collective-permute-done((f32[8,128,64]{2,1,0:T(8,128)}, f32[8,128,64]{2,1,0:T(8,128)S(1)}, u32[]{:S(2)}, u32[]{:S(2)}) %collective-permute-start) | collective-permute-done | bytes 262176 | tf_op jit(solution)/shard_map/while/body/eval_jaxpr/ppermute | solution.py:12
  277.4 11.2 %collective-permute-done = f32[8,128,64]{2,1,0:T(8,128)S(1)} collective-permute-done((f32[8,128,64]{2,1,0:T(8,128)}, f32[8,128,64]{2,1,0:T(8,128)S(1)}, u32[]{:S(2)}, u32[]{:S(2)}) %collective-permute-start) | collective-permute-done | bytes 262176 | tf_op jit(solution)/shard_map/while/body/eval_jaxpr/ppermute | solution.py:12
  316.6 8.4 collective-permute-done
  329.6 9.5 %collective-permute-done = f32[8,128,64]{2,1,0:T(8,128)S(1)} collective-permute-done((f32[8,128,64]{2,1,0:T(8,128)}, f32[8,128,64]{2,1,0:T(8,128)S(1)}, u32[]{:S(2)}, u32[]{:S(2)}) %collective-permute-start) | collective-permute-done | bytes 262176 | tf_op jit(solution)/shard_map/while/body/eval_jaxpr/ppermute | solution.py:12
  343.8 10.7 %collective-permute-done = f32[8,128,64]{2,1,0:T(8,128)S(1)} collective-permute-done((f32[8,128,64]{2,1,0:T(8,128)}, f32[8,128,64]{2,1,0:T(8,128)S(1)}, u32[]{:S(2)}, u32[]{:S(2)}) %collective-permute-start) | collective-permute-done | bytes 262176 | tf_op jit(solution)/shard_map/while/body/eval_jaxpr/ppermute | solution.py:12
  359.2 11.8 %collective-permute-done = f32[8,128,64]{2,1,0:T(8,128)S(1)} collective-permute-done((f32[8,128,64]{2,1,0:T(8,128)}, f32[8,128,64]{2,1,0:T(8,128)S(1)}, u32[]{:S(2)}, u32[]{:S(2)}) %collective-permute-start) | collective-permute-done | bytes 262176 | tf_op jit(solution)/shard_map/while/body/eval_jaxpr/ppermute | solution.py:12
  376.7 12.0 %collective-permute-done = f32[8,128,64]{2,1,0:T(8,128)S(1)} collective-permute-done((f32[8,128,64]{2,1,0:T(8,128)}, f32[8,128,64]{2,1,0:T(8,128)S(1)}, u32[]{:S(2)}, u32[]{:S(2)}) %collective-permute-start) | collective-permute-done | bytes 262176 | tf_op jit(solution)/shard_map/while/body/eval_jaxpr/ppermute | solution.py:12
  394.9 10.9 %collective-permute-done = f32[8,128,64]{2,1,0:T(8,128)S(1)} collective-permute-done((f32[8,128,64]{2,1,0:T(8,128)}, f32[8,128,64]{2,1,0:T(8,128)S(1)}, u32[]{:S(2)}, u32[]{:S(2)}) %collective-permute-start) | collective-permute-done | bytes 262176 | tf_op jit(solution)/shard_map/while/body/eval_jaxpr/ppermute | solution.py:12
  411.4 9.8 %collective-permute-done = f32[8,128,64]{2,1,0:T(8,128)S(1)} collective-permute-done((f32[8,128,64]{2,1,0:T(8,128)}, f32[8,128,64]{2,1,0:T(8,128)S(1)}, u32[]{:S(2)}, u32[]{:S(2)}) %collective-permute-start) | collective-permute-done | bytes 262176 | tf_op jit(solution)/shard_map/while/body/eval_jaxpr/ppermute | solution.py:12
  426.1 8.6 collective-permute-done
  440.9 7.8 collective-permute-done
  519.0 8.3 collective-permute-done
  533.0 8.7 collective-permute-done
  548.7 9.5 %collective-permute-done = f32[8,128,64]{2,1,0:T(8,128)S(1)} collective-permute-done((f32[8,128,64]{2,1,0:T(8,128)}, f32[8,128,64]{2,1,0:T(8,128)S(1)}, u32[]{:S(2)}, u32[]{:S(2)}) %collective-permute-start) | collective-permute-done | bytes 262176 | tf_op jit(solution)/shard_map/while/body/eval_jaxpr/ppermute | solution.py:12
  566.1 10.6 %collective-permute-done = f32[8,128,64]{2,1,0:T(8,128)S(1)} collective-permute-done((f32[8,128,64]{2,1,0:T(8,128)}, f32[8,128,64]{2,1,0:T(8,128)S(1)}, u32[]{:S(2)}, u32[]{:S(2)}) %collective-permute-start) | collective-permute-done | bytes 262176 | tf_op jit(solution)/shard_map/while/body/eval_jaxpr/ppermute | solution.py:12
  577.7 7.6 collective-permute-start
  585.3 11.8 %collective-permute-done = f32[8,128,64]{2,1,0:T(8,128)S(1)} collective-permute-done((f32[8,128,64]{2,1,0:T(8,128)}, f32[8,128,64]{2,1,0:T(8,128)S(1)}, u32[]{:S(2)}, u32[]{:S(2)}) %collective-permute-start) | collective-permute-done | bytes 262176 | tf_op jit(solution)/shard_map/while/body/eval_jaxpr/ppermute | solution.py:12
  598.0 7.7 collective-permute-start
  605.7 11.1 %collective-permute-done = f32[8,128,64]{2,1,0:T(8,128)S(1)} collective-permute-done((f32[8,128,64]{2,1,0:T(8,128)}, f32[8,128,64]{2,1,0:T(8,128)S(1)}, u32[]{:S(2)}, u32[]{:S(2)}) %collective-permute-start) | collective-permute-done | bytes 262176 | tf_op jit(solution)/shard_map/while/body/eval_jaxpr/ppermute | solution.py:12
  624.5 9.9 %collective-permute-done = f32[8,128,64]{2,1,0:T(8,128)S(1)} collective-permute-done((f32[8,128,64]{2,1,0:T(8,128)}, f32[8,128,64]{2,1,0:T(8,128)S(1)}, u32[]{:S(2)}, u32[]{:S(2)}) %collective-permute-start) | collective-permute-done | bytes 262176 | tf_op jit(solution)/shard_map/while/body/eval_jaxpr/ppermute | solution.py:12
  641.4 8.8 %collective-permute-done = f32[8,128,64]{2,1,0:T(8,128)S(1)} collective-permute-done((f32[8,128,64]{2,1,0:T(8,128)}, f32[8,128,64]{2,1,0:T(8,128)S(1)}, u32[]{:S(2)}, u32[]{:S(2)}) %collective-permute-start) | collective-permute-done | bytes 262176 | tf_op jit(solution)/shard_map/while/body/eval_jaxpr/ppermute | solution.py:12
  656.4 7.6 collective-permute-done
  700.5 15.3 %while.36 = (s32[]{:T(128)}, f32[8,128,64]{2,1,0:T(8,128)S(1)}, bf16[4,8,128,64]{3,2,1,0:T(8,128)(2,1)}, f32[4,8]{1,0:T(4,128)S(1)}, f32[4]{0:T(128)S(1)}, /*index=5*/f32[4,8,128,64]{3,2,1,0:T(8,128)}, s32[]{:T(128)}) while((s32[]{:T(128)}, f32[8,128,64]{2,1,0:T(8,128)S(1)}, bf16[4,8,128,64]{3,2,1,0:T(8,128)(2,1)}, f32[4,8]{1,0:T(4,128)S(1)}, ...), condition=%wide.region_9.10_spmd, body=%wide.region_8.9_spmd.sunk | while | flops 262146 | bytes 1574085 | solution.py:130
  737.1 48.3 %psum.7 = f32[1024]{0:T(1024)S(1)} all-reduce(f32[1024]{0:T(1024)S(1)} %get-tuple-element.196), channel_id=1, replica_groups=mesh['seq'=32,'tp'=8] {'tp'}, use_global_device_ids=true, to_apply=%region_11.12 | all-reduce | flops 1024 | bytes 8192 | tf_op jit(solution)/shard_map/psum | solution.py:139
  785.4 7.9 fusion.26
  794.3 72.8 %reduce-scatter.2.cloned.1.call-done = f32[1024,256]{1,0:T(8,128)} async-done(((f32[1024,2048]{1,0:T(8,128)}), f32[1024,256]{1,0:T(8,128)}) %reduce-scatter.2.cloned.1.call-update) | async-done | bytes 1048592 | tf_op jit(solution)/shard_map/reduce_scatter | solution.py:147
  (212 shorter events, 340.8 us)
Async XLA Ops:
  6.5 78.4 %all-gather.10.cloned.1.call-start = ((), (), s32[]{:S(2)}) async-start(), calls=%async_computation.3 | async-start | bytes 1081344 | tf_op jit(solution)/shard_map/all_gather | solution.py:67
  7.3 120.7 %all-gather.6.cloned.1.call-start = ((), (), s32[]{:S(2)}) async-start(), calls=%async_computation.1 | async-start | bytes 4718592 | tf_op jit(solution)/shard_map/all_gather | solution.py:64
  8.0 201.3 %all-gather.8.cloned.1.call-start = ((), (), s32[]{:S(2)}) async-start(), calls=%async_computation.2 | async-start | bytes 4325376 | tf_op jit(solution)/shard_map/all_gather | solution.py:66
  8.7 776.7 %all-gather.12.cloned.1.call-start = ((), (), s32[]{:S(2)}) async-start(), calls=%async_computation.4 | async-start | bytes 2162688 | tf_op jit(solution)/shard_map/all_gather | solution.py:144
  9.3 857.7 %reduce-scatter.2.cloned.1.call-start = ((), (), s32[]{:S(2)}) async-start(), calls=%async_computation.5 | async-start | bytes 9437184 | tf_op jit(solution)/shard_map/reduce_scatter | solution.py:147
  258.1 14.0 %collective-permute-start = (f32[8,128,64]{2,1,0:T(8,128)}, f32[8,128,64]{2,1,0:T(8,128)S(1)}, u32[]{:S(2)}, u32[]{:S(2)}) collective-permute-start(f32[8,128,64]{2,1,0:T(8,128)} %multiply_add_fusion.2), channel_id=1, source_target_pairs={{0,8},{8,16},{16,24},{24,32},{32,40},{40,48},{48,56},{56,64},{64,7... | collective-permute-start | bytes 786440 | tf_op jit(solution)/shard_map/while/body/eval_jaxpr/ppermute | solution.py:12
  273.0 15.6 %collective-permute-start = (f32[8,128,64]{2,1,0:T(8,128)}, f32[8,128,64]{2,1,0:T(8,128)S(1)}, u32[]{:S(2)}, u32[]{:S(2)}) collective-permute-start(f32[8,128,64]{2,1,0:T(8,128)} %multiply_add_fusion.2), channel_id=1, source_target_pairs={{0,8},{8,16},{16,24},{24,32},{32,40},{40,48},{48,56},{56,64},{64,7... | collective-permute-start | bytes 786440 | tf_op jit(solution)/shard_map/while/body/eval_jaxpr/ppermute | solution.py:12
  312.9 12.1 %collective-permute-start = (f32[8,128,64]{2,1,0:T(8,128)}, f32[8,128,64]{2,1,0:T(8,128)S(1)}, u32[]{:S(2)}, u32[]{:S(2)}) collective-permute-start(f32[8,128,64]{2,1,0:T(8,128)} %multiply_add_fusion.2), channel_id=1, source_target_pairs={{0,8},{8,16},{16,24},{24,32},{32,40},{40,48},{48,56},{56,64},{64,7... | collective-permute-start | bytes 786440 | tf_op jit(solution)/shard_map/while/body/eval_jaxpr/ppermute | solution.py:12
  325.9 13.3 %collective-permute-start = (f32[8,128,64]{2,1,0:T(8,128)}, f32[8,128,64]{2,1,0:T(8,128)S(1)}, u32[]{:S(2)}, u32[]{:S(2)}) collective-permute-start(f32[8,128,64]{2,1,0:T(8,128)} %multiply_add_fusion.2), channel_id=1, source_target_pairs={{0,8},{8,16},{16,24},{24,32},{32,40},{40,48},{48,56},{56,64},{64,7... | collective-permute-start | bytes 786440 | tf_op jit(solution)/shard_map/while/body/eval_jaxpr/ppermute | solution.py:12
  340.1 14.4 %collective-permute-start = (f32[8,128,64]{2,1,0:T(8,128)}, f32[8,128,64]{2,1,0:T(8,128)S(1)}, u32[]{:S(2)}, u32[]{:S(2)}) collective-permute-start(f32[8,128,64]{2,1,0:T(8,128)} %multiply_add_fusion.2), channel_id=1, source_target_pairs={{0,8},{8,16},{16,24},{24,32},{32,40},{40,48},{48,56},{56,64},{64,7... | collective-permute-start | bytes 786440 | tf_op jit(solution)/shard_map/while/body/eval_jaxpr/ppermute | solution.py:12
  355.4 15.6 %collective-permute-start = (f32[8,128,64]{2,1,0:T(8,128)}, f32[8,128,64]{2,1,0:T(8,128)S(1)}, u32[]{:S(2)}, u32[]{:S(2)}) collective-permute-start(f32[8,128,64]{2,1,0:T(8,128)} %multiply_add_fusion.2), channel_id=1, source_target_pairs={{0,8},{8,16},{16,24},{24,32},{32,40},{40,48},{48,56},{56,64},{64,7... | collective-permute-start | bytes 786440 | tf_op jit(solution)/shard_map/while/body/eval_jaxpr/ppermute | solution.py:12
  371.9 16.8 %collective-permute-start = (f32[8,128,64]{2,1,0:T(8,128)}, f32[8,128,64]{2,1,0:T(8,128)S(1)}, u32[]{:S(2)}, u32[]{:S(2)}) collective-permute-start(f32[8,128,64]{2,1,0:T(8,128)} %multiply_add_fusion.2), channel_id=1, source_target_pairs={{0,8},{8,16},{16,24},{24,32},{32,40},{40,48},{48,56},{56,64},{64,7... | collective-permute-start | bytes 786440 | tf_op jit(solution)/shard_map/while/body/eval_jaxpr/ppermute | solution.py:12
  389.6 16.3 %collective-permute-start = (f32[8,128,64]{2,1,0:T(8,128)}, f32[8,128,64]{2,1,0:T(8,128)S(1)}, u32[]{:S(2)}, u32[]{:S(2)}) collective-permute-start(f32[8,128,64]{2,1,0:T(8,128)} %multiply_add_fusion.2), channel_id=1, source_target_pairs={{0,8},{8,16},{16,24},{24,32},{32,40},{40,48},{48,56},{56,64},{64,7... | collective-permute-start | bytes 786440 | tf_op jit(solution)/shard_map/while/body/eval_jaxpr/ppermute | solution.py:12
  406.7 14.4 %collective-permute-start = (f32[8,128,64]{2,1,0:T(8,128)}, f32[8,128,64]{2,1,0:T(8,128)S(1)}, u32[]{:S(2)}, u32[]{:S(2)}) collective-permute-start(f32[8,128,64]{2,1,0:T(8,128)} %multiply_add_fusion.2), channel_id=1, source_target_pairs={{0,8},{8,16},{16,24},{24,32},{32,40},{40,48},{48,56},{56,64},{64,7... | collective-permute-start | bytes 786440 | tf_op jit(solution)/shard_map/while/body/eval_jaxpr/ppermute | solution.py:12
  422.1 12.7 %collective-permute-start = (f32[8,128,64]{2,1,0:T(8,128)}, f32[8,128,64]{2,1,0:T(8,128)S(1)}, u32[]{:S(2)}, u32[]{:S(2)}) collective-permute-start(f32[8,128,64]{2,1,0:T(8,128)} %multiply_add_fusion.2), channel_id=1, source_target_pairs={{0,8},{8,16},{16,24},{24,32},{32,40},{40,48},{48,56},{56,64},{64,7... | collective-permute-start | bytes 786440 | tf_op jit(solution)/shard_map/while/body/eval_jaxpr/ppermute | solution.py:12
  435.7 13.0 %collective-permute-start = (f32[8,128,64]{2,1,0:T(8,128)}, f32[8,128,64]{2,1,0:T(8,128)S(1)}, u32[]{:S(2)}, u32[]{:S(2)}) collective-permute-start(f32[8,128,64]{2,1,0:T(8,128)} %multiply_add_fusion.2), channel_id=1, source_target_pairs={{0,8},{8,16},{16,24},{24,32},{32,40},{40,48},{48,56},{56,64},{64,7... | collective-permute-start | bytes 786440 | tf_op jit(solution)/shard_map/while/body/eval_jaxpr/ppermute | solution.py:12
  449.6 12.2 %collective-permute-start = (f32[8,128,64]{2,1,0:T(8,128)}, f32[8,128,64]{2,1,0:T(8,128)S(1)}, u32[]{:S(2)}, u32[]{:S(2)}) collective-permute-start(f32[8,128,64]{2,1,0:T(8,128)} %multiply_add_fusion.2), channel_id=1, source_target_pairs={{0,8},{8,16},{16,24},{24,32},{32,40},{40,48},{48,56},{56,64},{64,7... | collective-permute-start | bytes 786440 | tf_op jit(solution)/shard_map/while/body/eval_jaxpr/ppermute | solution.py:12
  462.7 11.6 %collective-permute-start = (f32[8,128,64]{2,1,0:T(8,128)}, f32[8,128,64]{2,1,0:T(8,128)S(1)}, u32[]{:S(2)}, u32[]{:S(2)}) collective-permute-start(f32[8,128,64]{2,1,0:T(8,128)} %multiply_add_fusion.2), channel_id=1, source_target_pairs={{0,8},{8,16},{16,24},{24,32},{32,40},{40,48},{48,56},{56,64},{64,7... | collective-permute-start | bytes 786440 | tf_op jit(solution)/shard_map/while/body/eval_jaxpr/ppermute | solution.py:12
  475.2 11.6 %collective-permute-start = (f32[8,128,64]{2,1,0:T(8,128)}, f32[8,128,64]{2,1,0:T(8,128)S(1)}, u32[]{:S(2)}, u32[]{:S(2)}) collective-permute-start(f32[8,128,64]{2,1,0:T(8,128)} %multiply_add_fusion.2), channel_id=1, source_target_pairs={{0,8},{8,16},{16,24},{24,32},{32,40},{40,48},{48,56},{56,64},{64,7... | collective-permute-start | bytes 786440 | tf_op jit(solution)/shard_map/while/body/eval_jaxpr/ppermute | solution.py:12
  487.7 11.6 %collective-permute-start = (f32[8,128,64]{2,1,0:T(8,128)}, f32[8,128,64]{2,1,0:T(8,128)S(1)}, u32[]{:S(2)}, u32[]{:S(2)}) collective-permute-start(f32[8,128,64]{2,1,0:T(8,128)} %multiply_add_fusion.2), channel_id=1, source_target_pairs={{0,8},{8,16},{16,24},{24,32},{32,40},{40,48},{48,56},{56,64},{64,7... | collective-permute-start | bytes 786440 | tf_op jit(solution)/shard_map/while/body/eval_jaxpr/ppermute | solution.py:12
  500.3 12.4 %collective-permute-start = (f32[8,128,64]{2,1,0:T(8,128)}, f32[8,128,64]{2,1,0:T(8,128)S(1)}, u32[]{:S(2)}, u32[]{:S(2)}) collective-permute-start(f32[8,128,64]{2,1,0:T(8,128)} %multiply_add_fusion.2), channel_id=1, source_target_pairs={{0,8},{8,16},{16,24},{24,32},{32,40},{40,48},{48,56},{56,64},{64,7... | collective-permute-start | bytes 786440 | tf_op jit(solution)/shard_map/while/body/eval_jaxpr/ppermute | solution.py:12
  513.5 13.7 %collective-permute-start = (f32[8,128,64]{2,1,0:T(8,128)}, f32[8,128,64]{2,1,0:T(8,128)S(1)}, u32[]{:S(2)}, u32[]{:S(2)}) collective-permute-start(f32[8,128,64]{2,1,0:T(8,128)} %multiply_add_fusion.2), channel_id=1, source_target_pairs={{0,8},{8,16},{16,24},{24,32},{32,40},{40,48},{48,56},{56,64},{64,7... | collective-permute-start | bytes 786440 | tf_op jit(solution)/shard_map/while/body/eval_jaxpr/ppermute | solution.py:12
  528.1 13.5 %collective-permute-start = (f32[8,128,64]{2,1,0:T(8,128)}, f32[8,128,64]{2,1,0:T(8,128)S(1)}, u32[]{:S(2)}, u32[]{:S(2)}) collective-permute-start(f32[8,128,64]{2,1,0:T(8,128)} %multiply_add_fusion.2), channel_id=1, source_target_pairs={{0,8},{8,16},{16,24},{24,32},{32,40},{40,48},{48,56},{56,64},{64,7... | collective-permute-start | bytes 786440 | tf_op jit(solution)/shard_map/while/body/eval_jaxpr/ppermute | solution.py:12
  542.5 15.6 %collective-permute-start = (f32[8,128,64]{2,1,0:T(8,128)}, f32[8,128,64]{2,1,0:T(8,128)S(1)}, u32[]{:S(2)}, u32[]{:S(2)}) collective-permute-start(f32[8,128,64]{2,1,0:T(8,128)} %multiply_add_fusion.2), channel_id=1, source_target_pairs={{0,8},{8,16},{16,24},{24,32},{32,40},{40,48},{48,56},{56,64},{64,7... | collective-permute-start | bytes 786440 | tf_op jit(solution)/shard_map/while/body/eval_jaxpr/ppermute | solution.py:12
  559.1 17.7 %collective-permute-start = (f32[8,128,64]{2,1,0:T(8,128)}, f32[8,128,64]{2,1,0:T(8,128)S(1)}, u32[]{:S(2)}, u32[]{:S(2)}) collective-permute-start(f32[8,128,64]{2,1,0:T(8,128)} %multiply_add_fusion.2), channel_id=1, source_target_pairs={{0,8},{8,16},{16,24},{24,32},{32,40},{40,48},{48,56},{56,64},{64,7... | collective-permute-start | bytes 786440 | tf_op jit(solution)/shard_map/while/body/eval_jaxpr/ppermute | solution.py:12
  577.7 19.4 %collective-permute-start = (f32[8,128,64]{2,1,0:T(8,128)}, f32[8,128,64]{2,1,0:T(8,128)S(1)}, u32[]{:S(2)}, u32[]{:S(2)}) collective-permute-start(f32[8,128,64]{2,1,0:T(8,128)} %multiply_add_fusion.2), channel_id=1, source_target_pairs={{0,8},{8,16},{16,24},{24,32},{32,40},{40,48},{48,56},{56,64},{64,7... | collective-permute-start | bytes 786440 | tf_op jit(solution)/shard_map/while/body/eval_jaxpr/ppermute | solution.py:12
  598.0 18.8 %collective-permute-start = (f32[8,128,64]{2,1,0:T(8,128)}, f32[8,128,64]{2,1,0:T(8,128)S(1)}, u32[]{:S(2)}, u32[]{:S(2)}) collective-permute-start(f32[8,128,64]{2,1,0:T(8,128)} %multiply_add_fusion.2), channel_id=1, source_target_pairs={{0,8},{8,16},{16,24},{24,32},{32,40},{40,48},{48,56},{56,64},{64,7... | collective-permute-start | bytes 786440 | tf_op jit(solution)/shard_map/while/body/eval_jaxpr/ppermute | solution.py:12
  617.7 16.6 %collective-permute-start = (f32[8,128,64]{2,1,0:T(8,128)}, f32[8,128,64]{2,1,0:T(8,128)S(1)}, u32[]{:S(2)}, u32[]{:S(2)}) collective-permute-start(f32[8,128,64]{2,1,0:T(8,128)} %multiply_add_fusion.2), channel_id=1, source_target_pairs={{0,8},{8,16},{16,24},{24,32},{32,40},{40,48},{48,56},{56,64},{64,7... | collective-permute-start | bytes 786440 | tf_op jit(solution)/shard_map/while/body/eval_jaxpr/ppermute | solution.py:12
  635.3 14.9 %collective-permute-start = (f32[8,128,64]{2,1,0:T(8,128)}, f32[8,128,64]{2,1,0:T(8,128)S(1)}, u32[]{:S(2)}, u32[]{:S(2)}) collective-permute-start(f32[8,128,64]{2,1,0:T(8,128)} %multiply_add_fusion.2), channel_id=1, source_target_pairs={{0,8},{8,16},{16,24},{24,32},{32,40},{40,48},{48,56},{56,64},{64,7... | collective-permute-start | bytes 786440 | tf_op jit(solution)/shard_map/while/body/eval_jaxpr/ppermute | solution.py:12
  651.1 12.9 %collective-permute-start = (f32[8,128,64]{2,1,0:T(8,128)}, f32[8,128,64]{2,1,0:T(8,128)S(1)}, u32[]{:S(2)}, u32[]{:S(2)}) collective-permute-start(f32[8,128,64]{2,1,0:T(8,128)} %multiply_add_fusion.2), channel_id=1, source_target_pairs={{0,8},{8,16},{16,24},{24,32},{32,40},{40,48},{48,56},{56,64},{64,7... | collective-permute-start | bytes 786440 | tf_op jit(solution)/shard_map/while/body/eval_jaxpr/ppermute | solution.py:12
  676.6 11.6 %collective-permute-start = (f32[8,128,64]{2,1,0:T(8,128)}, f32[8,128,64]{2,1,0:T(8,128)S(1)}, u32[]{:S(2)}, u32[]{:S(2)}) collective-permute-start(f32[8,128,64]{2,1,0:T(8,128)} %multiply_add_fusion.2), channel_id=1, source_target_pairs={{0,8},{8,16},{16,24},{24,32},{32,40},{40,48},{48,56},{56,64},{64,7... | collective-permute-start | bytes 786440 | tf_op jit(solution)/shard_map/while/body/eval_jaxpr/ppermute | solution.py:12
  689.1 11.4 %collective-permute-start = (f32[8,128,64]{2,1,0:T(8,128)}, f32[8,128,64]{2,1,0:T(8,128)S(1)}, u32[]{:S(2)}, u32[]{:S(2)}) collective-permute-start(f32[8,128,64]{2,1,0:T(8,128)} %multiply_add_fusion.2), channel_id=1, source_target_pairs={{0,8},{8,16},{16,24},{24,32},{32,40},{40,48},{48,56},{56,64},{64,7... | collective-permute-start | bytes 786440 | tf_op jit(solution)/shard_map/while/body/eval_jaxpr/ppermute | solution.py:12
  (27 other events, 1237.1 us)
Sparse Core Ops, SparseCore 0:
  9.9 75.0 all-gather.9
  86.8 41.0 all-gather.5
  130.5 78.7 all-gather.7
  211.7 75.2 all-gather.11
  793.5 73.4 reduce-scatter.1
where the time goes:
time: 878 us; the launch traced here: 876 us
  waiting for transfers between devices  483 us (55%)
  starting transfers between devices  162 us (18%)
  blocking collectives  90.2 us (10%)
  other arithmetic  68 us (8%)
  local copies, waits for them, and re-layouts  29.4 us (3%)
  matrix products  28.5 us (3%)
  between operations  13.5 us (2%)
    ppermute x33, waiting for transfers between devices, passed_along(): return lax.ppermute(value, axis, pairs)  270 us
    ppermute x33, starting transfers between devices, passed_along(): return lax.ppermute(value, axis, pairs)  162 us
    reduce_scatter x1, waiting for transfers between devices, on_device(): lax.psum_scatter(partial_out, 'tp', scatter_dimension=1, tiled=True)  72.8 us
    all_gather x1, waiting for transfers between devices, on_device(): lax.all_gather(w_inner, 'seq', axis=0, tiled=True)  67.3 us
    psum x1, blocking collectives, on_device(): squares = lax.psum(jnp.sum(gated * gated, axis=1), 'tp')  48.3 us
    all_gather x1, waiting for transfers between devices, on_device(): whole = lax.all_gather(tokens, 'tp', axis=1, tiled=True)  42.9 us
    all_gather x1, blocking collectives, on_device(): lax.all_gather(w_step, 'seq', axis=0, tiled=True)  41.9 us
    add x31, other arithmetic, relay(): block_gain[:, None, None] * entering_now + block_state  28.2 us
  transfers between devices with their start and end apart: 38, of which 35 were waited for; matrix products, arithmetic and copies ran while one was open for 13% of the time, Pallas kernels for 0%

commit v1 on v0

--- a/solution.py
+++ b/solution.py
@@ -4,6 +4,27 @@
 from jax.sharding import PartitionSpec as P
 
 BLOCK = 256
+
+
+def collect(shard, axis, dim):
+    size, index, span = (lax.axis_size(axis), lax.axis_index(axis), shard.shape[dim])
+    forward = [(i, (i + 1) % size) for i in range(size)]
+    left = [(i, (i - 1) % size) for i in range(size)]
+    out = jnp.zeros((*shard.shape[:dim], size * span, *shard.shape[dim + 1 :]), shard.dtype)
+    out = lax.dynamic_update_slice_in_dim(out, shard, index * span, axis=dim)
+    from_left = from_right = shard
+    middle = size // 2
+    for step in range(1, middle + 1):
+        from_left = lax.ppermute(from_left, axis, forward)
+        out = lax.dynamic_update_slice_in_dim(
+            out, from_left, (index - step) % size * span, axis=dim
+        )
+        if step < size - middle:
+            from_right = lax.ppermute(from_right, axis, left)
+            out = lax.dynamic_update_slice_in_dim(
+                out, from_right, (index + step) % size * span, axis=dim
+            )
+    return out
 
 
 def passed_along(value, axis, by):
@@ -61,7 +82,7 @@
     local_valid = lax.dynamic_slice_in_dim(valid_rows, seq_index * local_blocks, local_blocks)
     in_block = jnp.arange(row_count, dtype=jnp.int32) % BLOCK
     carry_on = jnp.repeat(local_start == 0, BLOCK)
-    whole = lax.all_gather(tokens, "tp", axis=1, tiled=True)
+    whole = collect(tokens, "tp", 1)
     pieces = (
         lax.all_gather(w_inner, "seq", axis=0, tiled=True),
         lax.all_gather(w_states, "seq", axis=0, tiled=True),

time: 878 us -> 841 us (0.958)
  waiting for transfers between devices: 483 us -> 414 us
  starting transfers between devices: 162 us -> 182 us
  local copies, waits for them, and re-layouts: 29.4 us -> 38.2 us
    all_gather x1 -> x0, waiting for transfers between devices: 42.9 us -> none  [on_device(): whole = lax.all_gather(tokens, 'tp', axis=1, tiled=True)]
    all_gather x1, waiting for transfers between devices: 27.5 us -> 0.01 us  [on_device(): lax.all_gather(w_states, 'seq', axis=0, tiled=True)]
    ppermute x0 -> x7, starting transfers between devices: none -> 22.2 us  [the longest x3 14.7 us: collect(): from_right = lax.ppermute(from_right, axis, left)]
    all_gather x1, waiting for transfers between devices: 67.3 us -> 57.5 us  [on_device(): lax.all_gather(w_inner, 'seq', axis=0, tiled=True)]
    ppermute x0 -> x7, waiting for transfers between devices: none -> 8.92 us  [the longest x4 7.38 us: collect(): from_left = lax.ppermute(from_left, axis, forward)]
  transfers between devices with their start and end apart: 38 -> 44, of which waited for: 35 -> 37; matrix products, arithmetic and copies ran while one was open for 13% -> 15% of each run, Pallas kernels for 0% -> 0%
where the time goes in v1:
time: 841 us; the launch traced here: 839 us
  waiting for transfers between devices  414 us (49%)
  starting transfers between devices  182 us (22%)
  blocking collectives  89.9 us (11%)
  other arithmetic  68.2 us (8%)
  local copies, waits for them, and re-layouts  38.2 us (5%)
  matrix products  32.7 us (4%)
  between operations  13.6 us (2%)
    ppermute x33, waiting for transfers between devices, passed_along(): return lax.ppermute(value, axis, pairs)  272 us
    ppermute x33, starting transfers between devices, passed_along(): return lax.ppermute(value, axis, pairs)  159 us
    reduce_scatter x1, waiting for transfers between devices, on_device(): lax.psum_scatter(partial_out, 'tp', scatter_dimension=1, tiled=True)  73.8 us
    all_gather x1, waiting for transfers between devices, on_device(): lax.all_gather(w_inner, 'seq', axis=0, tiled=True)  57.5 us
    psum x1, blocking collectives, on_device(): squares = lax.psum(jnp.sum(gated * gated, axis=1), 'tp')  48.9 us
    all_gather x1, blocking collectives, on_device(): lax.all_gather(w_step, 'seq', axis=0, tiled=True)  40.9 us
    add x31, other arithmetic, relay(): block_gain[:, None, None] * entering_now + block_state  28.2 us
  transfers between devices with their start and end apart: 44, of which 37 were waited for; matrix products, arithmetic and copies ran while one was open for 15% of the time, Pallas kernels for 0%

profile of v1, /device:TPU:1, one launch (start us, length us, event | category | flops | bytes accessed | tf_op | source)
XLA Modules:
  0.0 839.0 jit_solution(11360892853145548981)
XLA Ops:
  28.3 40.9 %all-gather = bf16[32,64,8]{1,2,0:T(8,128)(2,1)S(1)} all-gather(bf16[1,64,8]{1,2,0:T(8,128)(2,1)} %bitcast.99), channel_id=1, replica_groups=mesh['seq'=32,'tp'=8] {'seq'}, dimensions={0}, use_global_device_ids=true | all-gather | bytes 33792 | tf_op jit(solution)/shard_map/all_gather | solution.py:89
  74.9 12.4 %collective-permute-start.6 = (bf16[1024,256]{1,0:T(8,128)(2,1)S(1)}, bf16[1024,256]{1,0:T(8,128)(2,1)S(1)}, u32[]{:S(2)}, u32[]{:S(2)}) collective-permute-start(bf16[1024,256]{1,0:T(8,128)(2,1)S(1)} %collective-permute-done.4), channel_id=1, source_target_pairs={{0,7},{1,0},{2,1},{3,2},{4,3},{5,4},{6,5},{7,6},{8,15},{9,8},{10,9... | collective-permute-start | bytes 1572872 | tf_op jit(solution)/shard_map/ppermute | solution.py:23
  110.8 57.5 %all-gather.5.cloned.1.call-done = bf16[2048,2,512]{2,1,0:T(2,128)(2,1)} async-done(((bf16[64,2,512]{2,1,0:T(2,128)(2,1)}), bf16[2048,2,512]{2,1,0:T(2,128)(2,1)}) %all-gather.5.cloned.1.call-update) | async-done | bytes 4194320 | tf_op jit(solution)/shard_map/all_gather | solution.py:87
  199.6 7.5 while.37
  207.1 454.8 %while.35 = (s32[]{:T(128)}, f32[8,128,64]{2,1,0:T(8,128)S(1)}, f32[8]{0:T(128)S(1)}, f32[8,128,64]{2,1,0:T(8,128)S(1)}, s32[]{:T(128)}) while((s32[]{:T(128)}, f32[8,128,64]{2,1,0:T(8,128)S(1)}, f32[8]{0:T(128)S(1)}, f32[8,128,64]{2,1,0:T(8,128)S(1)}, s32[]{:T(128)}) %tuple.77), condition=%wide.region_7.8_spmd, body=%wide.region_6.7_spmd.sunk | while | flops 131074 | bytes 1835141 | solution.py:144
  211.4 7.7 collective-permute-done
  224.1 11.4 %collective-permute-done = f32[8,128,64]{2,1,0:T(8,128)S(1)} collective-permute-done((f32[8,128,64]{2,1,0:T(8,128)}, f32[8,128,64]{2,1,0:T(8,128)S(1)}, u32[]{:S(2)}, u32[]{:S(2)}) %collective-permute-start) | collective-permute-done | bytes 262176 | tf_op jit(solution)/shard_map/while/body/eval_jaxpr/ppermute | solution.py:33
  240.4 9.8 %collective-permute-done = f32[8,128,64]{2,1,0:T(8,128)S(1)} collective-permute-done((f32[8,128,64]{2,1,0:T(8,128)}, f32[8,128,64]{2,1,0:T(8,128)S(1)}, u32[]{:S(2)}, u32[]{:S(2)}) %collective-permute-start) | collective-permute-done | bytes 262176 | tf_op jit(solution)/shard_map/while/body/eval_jaxpr/ppermute | solution.py:33
  266.4 8.2 collective-permute-done
  279.4 9.7 %collective-permute-done = f32[8,128,64]{2,1,0:T(8,128)S(1)} collective-permute-done((f32[8,128,64]{2,1,0:T(8,128)}, f32[8,128,64]{2,1,0:T(8,128)S(1)}, u32[]{:S(2)}, u32[]{:S(2)}) %collective-permute-start) | collective-permute-done | bytes 262176 | tf_op jit(solution)/shard_map/while/body/eval_jaxpr/ppermute | solution.py:33
  294.4 10.9 %collective-permute-done = f32[8,128,64]{2,1,0:T(8,128)S(1)} collective-permute-done((f32[8,128,64]{2,1,0:T(8,128)}, f32[8,128,64]{2,1,0:T(8,128)S(1)}, u32[]{:S(2)}, u32[]{:S(2)}) %collective-permute-start) | collective-permute-done | bytes 262176 | tf_op jit(solution)/shard_map/while/body/eval_jaxpr/ppermute | solution.py:33
  310.3 11.8 %collective-permute-done = f32[8,128,64]{2,1,0:T(8,128)S(1)} collective-permute-done((f32[8,128,64]{2,1,0:T(8,128)}, f32[8,128,64]{2,1,0:T(8,128)S(1)}, u32[]{:S(2)}, u32[]{:S(2)}) %collective-permute-start) | collective-permute-done | bytes 262176 | tf_op jit(solution)/shard_map/while/body/eval_jaxpr/ppermute | solution.py:33
  327.1 11.3 %collective-permute-done = f32[8,128,64]{2,1,0:T(8,128)S(1)} collective-permute-done((f32[8,128,64]{2,1,0:T(8,128)}, f32[8,128,64]{2,1,0:T(8,128)S(1)}, u32[]{:S(2)}, u32[]{:S(2)}) %collective-permute-start) | collective-permute-done | bytes 262176 | tf_op jit(solution)/shard_map/while/body/eval_jaxpr/ppermute | solution.py:33
  344.2 10.8 %collective-permute-done = f32[8,128,64]{2,1,0:T(8,128)S(1)} collective-permute-done((f32[8,128,64]{2,1,0:T(8,128)}, f32[8,128,64]{2,1,0:T(8,128)S(1)}, u32[]{:S(2)}, u32[]{:S(2)}) %collective-permute-start) | collective-permute-done | bytes 262176 | tf_op jit(solution)/shard_map/while/body/eval_jaxpr/ppermute | solution.py:33
  360.5 9.7 %collective-permute-done = f32[8,128,64]{2,1,0:T(8,128)S(1)} collective-permute-done((f32[8,128,64]{2,1,0:T(8,128)}, f32[8,128,64]{2,1,0:T(8,128)S(1)}, u32[]{:S(2)}, u32[]{:S(2)}) %collective-permute-start) | collective-permute-done | bytes 262176 | tf_op jit(solution)/shard_map/while/body/eval_jaxpr/ppermute | solution.py:33
  375.4 8.6 %collective-permute-done = f32[8,128,64]{2,1,0:T(8,128)S(1)} collective-permute-done((f32[8,128,64]{2,1,0:T(8,128)}, f32[8,128,64]{2,1,0:T(8,128)S(1)}, u32[]{:S(2)}, u32[]{:S(2)}) %collective-permute-start) | collective-permute-done | bytes 262176 | tf_op jit(solution)/shard_map/while/body/eval_jaxpr/ppermute | solution.py:33
  390.2 7.7 collective-permute-done
  454.7 7.2 collective-permute-done
  468.2 8.3 collective-permute-done
  483.3 9.5 %collective-permute-done = f32[8,128,64]{2,1,0:T(8,128)S(1)} collective-permute-done((f32[8,128,64]{2,1,0:T(8,128)}, f32[8,128,64]{2,1,0:T(8,128)S(1)}, u32[]{:S(2)}, u32[]{:S(2)}) %collective-permute-start) | collective-permute-done | bytes 262176 | tf_op jit(solution)/shard_map/while/body/eval_jaxpr/ppermute | solution.py:33
  498.7 10.2 %collective-permute-done = f32[8,128,64]{2,1,0:T(8,128)S(1)} collective-permute-done((f32[8,128,64]{2,1,0:T(8,128)}, f32[8,128,64]{2,1,0:T(8,128)S(1)}, u32[]{:S(2)}, u32[]{:S(2)}) %collective-permute-start) | collective-permute-done | bytes 262176 | tf_op jit(solution)/shard_map/while/body/eval_jaxpr/ppermute | solution.py:33
  515.2 11.1 %collective-permute-done = f32[8,128,64]{2,1,0:T(8,128)S(1)} collective-permute-done((f32[8,128,64]{2,1,0:T(8,128)}, f32[8,128,64]{2,1,0:T(8,128)S(1)}, u32[]{:S(2)}, u32[]{:S(2)}) %collective-permute-start) | collective-permute-done | bytes 262176 | tf_op jit(solution)/shard_map/while/body/eval_jaxpr/ppermute | solution.py:33
  532.0 11.6 %collective-permute-done = f32[8,128,64]{2,1,0:T(8,128)S(1)} collective-permute-done((f32[8,128,64]{2,1,0:T(8,128)}, f32[8,128,64]{2,1,0:T(8,128)S(1)}, u32[]{:S(2)}, u32[]{:S(2)}) %collective-permute-start) | collective-permute-done | bytes 262176 | tf_op jit(solution)/shard_map/while/body/eval_jaxpr/ppermute | solution.py:33
  544.5 7.9 collective-permute-start
  552.4 11.3 %collective-permute-done = f32[8,128,64]{2,1,0:T(8,128)S(1)} collective-permute-done((f32[8,128,64]{2,1,0:T(8,128)}, f32[8,128,64]{2,1,0:T(8,128)S(1)}, u32[]{:S(2)}, u32[]{:S(2)}) %collective-permute-start) | collective-permute-done | bytes 262176 | tf_op jit(solution)/shard_map/while/body/eval_jaxpr/ppermute | solution.py:33
  571.5 10.1 %collective-permute-done = f32[8,128,64]{2,1,0:T(8,128)S(1)} collective-permute-done((f32[8,128,64]{2,1,0:T(8,128)}, f32[8,128,64]{2,1,0:T(8,128)S(1)}, u32[]{:S(2)}, u32[]{:S(2)}) %collective-permute-start) | collective-permute-done | bytes 262176 | tf_op jit(solution)/shard_map/while/body/eval_jaxpr/ppermute | solution.py:33
  588.7 9.0 %collective-permute-done = f32[8,128,64]{2,1,0:T(8,128)S(1)} collective-permute-done((f32[8,128,64]{2,1,0:T(8,128)}, f32[8,128,64]{2,1,0:T(8,128)S(1)}, u32[]{:S(2)}, u32[]{:S(2)}) %collective-permute-start) | collective-permute-done | bytes 262176 | tf_op jit(solution)/shard_map/while/body/eval_jaxpr/ppermute | solution.py:33
  604.1 7.8 collective-permute-done
  661.9 15.3 %while.36 = (s32[]{:T(128)}, f32[8,128,64]{2,1,0:T(8,128)S(1)}, bf16[4,8,128,64]{3,2,1,0:T(8,128)(2,1)}, f32[4,8]{1,0:T(4,128)S(1)}, f32[4]{0:T(128)S(1)}, /*index=5*/f32[4,8,128,64]{3,2,1,0:T(8,128)}, s32[]{:T(128)}) while((s32[]{:T(128)}, f32[8,128,64]{2,1,0:T(8,128)S(1)}, bf16[4,8,128,64]{3,2,1,0:T(8,128)(2,1)}, f32[4,8]{1,0:T(4,128)S(1)}, ...), condition=%wide.region_9.10_spmd, body=%wide.region_8.9_spmd.sunk | while | flops 262146 | bytes 1574085 | solution.py:151
  698.6 48.9 %psum.7 = f32[1024]{0:T(1024)S(1)} all-reduce(f32[1024]{0:T(1024)S(1)} %get-tuple-element.196), channel_id=1, replica_groups=mesh['seq'=32,'tp'=8] {'tp'}, use_global_device_ids=true, to_apply=%region_11.12 | all-reduce | flops 1024 | bytes 8192 | tf_op jit(solution)/shard_map/psum | solution.py:160
  747.6 7.9 fusion.26
  756.4 73.8 %reduce-scatter.2.cloned.1.call-done = f32[1024,256]{1,0:T(8,128)} async-done(((f32[1024,2048]{1,0:T(8,128)}), f32[1024,256]{1,0:T(8,128)}) %reduce-scatter.2.cloned.1.call-update) | async-done | bytes 1048592 | tf_op jit(solution)/shard_map/reduce_scatter | solution.py:168
  (236 shorter events, 361.9 us)
Async XLA Ops:
  6.5 88.7 %all-gather.7.cloned.1.call-start = ((), (), s32[]{:S(2)}) async-start(), calls=%async_computation.2 | async-start | bytes 1081344 | tf_op jit(solution)/shard_map/all_gather | solution.py:88
  7.3 161.1 %all-gather.5.cloned.1.call-start = ((), (), s32[]{:S(2)}) async-start(), calls=%async_computation.1 | async-start | bytes 4325376 | tf_op jit(solution)/shard_map/all_gather | solution.py:87
  8.0 739.6 %all-gather.9.cloned.1.call-start = ((), (), s32[]{:S(2)}) async-start(), calls=%async_computation.3 | async-start | bytes 2162688 | tf_op jit(solution)/shard_map/all_gather | solution.py:165
  11.3 818.9 %reduce-scatter.2.cloned.1.call-start = ((), (), s32[]{:S(2)}) async-start(), calls=%async_computation.4 | async-start | bytes 9437184 | tf_op jit(solution)/shard_map/reduce_scatter | solution.py:168
  20.4 54.5 %collective-permute-start.4 = (bf16[1024,256]{1,0:T(8,128)(2,1)S(1)}, bf16[1024,256]{1,0:T(8,128)(2,1)S(1)}, u32[]{:S(2)}, u32[]{:S(2)}) collective-permute-start(bf16[1024,256]{1,0:T(8,128)(2,1)S(1)} %collective-permute-done.2), channel_id=1, source_target_pairs={{0,7},{1,0},{2,1},{3,2},{4,3},{5,4},{6,5},{7,6},{8,15},{9,8},{10,9... | collective-permute-start | bytes 1572872 | tf_op jit(solution)/shard_map/ppermute | solution.py:23
  25.7 62.5 %collective-permute-start.5 = (bf16[1024,256]{1,0:T(8,128)(2,1)S(1)}, bf16[1024,256]{1,0:T(8,128)(2,1)S(1)}, u32[]{:S(2)}, u32[]{:S(2)}) collective-permute-start(bf16[1024,256]{1,0:T(8,128)(2,1)S(1)} %collective-permute-done.3), channel_id=1, source_target_pairs={{0,1},{1,2},{2,3},{3,4},{4,5},{5,6},{6,7},{7,0},{8,9},{9,10},{10,1... | collective-permute-start | bytes 1572872 | tf_op jit(solution)/shard_map/ppermute | solution.py:18
  74.9 18.3 %collective-permute-start.6 = (bf16[1024,256]{1,0:T(8,128)(2,1)S(1)}, bf16[1024,256]{1,0:T(8,128)(2,1)S(1)}, u32[]{:S(2)}, u32[]{:S(2)}) collective-permute-start(bf16[1024,256]{1,0:T(8,128)(2,1)S(1)} %collective-permute-done.4), channel_id=1, source_target_pairs={{0,7},{1,0},{2,1},{3,2},{4,3},{5,4},{6,5},{7,6},{8,15},{9,8},{10,9... | collective-permute-start | bytes 1572872 | tf_op jit(solution)/shard_map/ppermute | solution.py:23
  220.0 15.4 %collective-permute-start = (f32[8,128,64]{2,1,0:T(8,128)}, f32[8,128,64]{2,1,0:T(8,128)S(1)}, u32[]{:S(2)}, u32[]{:S(2)}) collective-permute-start(f32[8,128,64]{2,1,0:T(8,128)} %multiply_add_fusion.2), channel_id=1, source_target_pairs={{0,8},{8,16},{16,24},{24,32},{32,40},{40,48},{48,56},{56,64},{64,7... | collective-permute-start | bytes 786440 | tf_op jit(solution)/shard_map/while/body/eval_jaxpr/ppermute | solution.py:33
  236.3 13.8 %collective-permute-start = (f32[8,128,64]{2,1,0:T(8,128)}, f32[8,128,64]{2,1,0:T(8,128)S(1)}, u32[]{:S(2)}, u32[]{:S(2)}) collective-permute-start(f32[8,128,64]{2,1,0:T(8,128)} %multiply_add_fusion.2), channel_id=1, source_target_pairs={{0,8},{8,16},{16,24},{24,32},{32,40},{40,48},{48,56},{56,64},{64,7... | collective-permute-start | bytes 786440 | tf_op jit(solution)/shard_map/while/body/eval_jaxpr/ppermute | solution.py:33
  262.7 11.9 %collective-permute-start = (f32[8,128,64]{2,1,0:T(8,128)}, f32[8,128,64]{2,1,0:T(8,128)S(1)}, u32[]{:S(2)}, u32[]{:S(2)}) collective-permute-start(f32[8,128,64]{2,1,0:T(8,128)} %multiply_add_fusion.2), channel_id=1, source_target_pairs={{0,8},{8,16},{16,24},{24,32},{32,40},{40,48},{48,56},{56,64},{64,7... | collective-permute-start | bytes 786440 | tf_op jit(solution)/shard_map/while/body/eval_jaxpr/ppermute | solution.py:33
  275.5 13.6 %collective-permute-start = (f32[8,128,64]{2,1,0:T(8,128)}, f32[8,128,64]{2,1,0:T(8,128)S(1)}, u32[]{:S(2)}, u32[]{:S(2)}) collective-permute-start(f32[8,128,64]{2,1,0:T(8,128)} %multiply_add_fusion.2), channel_id=1, source_target_pairs={{0,8},{8,16},{16,24},{24,32},{32,40},{40,48},{48,56},{56,64},{64,7... | collective-permute-start | bytes 786440 | tf_op jit(solution)/shard_map/while/body/eval_jaxpr/ppermute | solution.py:33
  290.0 15.2 %collective-permute-start = (f32[8,128,64]{2,1,0:T(8,128)}, f32[8,128,64]{2,1,0:T(8,128)S(1)}, u32[]{:S(2)}, u32[]{:S(2)}) collective-permute-start(f32[8,128,64]{2,1,0:T(8,128)} %multiply_add_fusion.2), channel_id=1, source_target_pairs={{0,8},{8,16},{16,24},{24,32},{32,40},{40,48},{48,56},{56,64},{64,7... | collective-permute-start | bytes 786440 | tf_op jit(solution)/shard_map/while/body/eval_jaxpr/ppermute | solution.py:33
  306.1 16.0 %collective-permute-start = (f32[8,128,64]{2,1,0:T(8,128)}, f32[8,128,64]{2,1,0:T(8,128)S(1)}, u32[]{:S(2)}, u32[]{:S(2)}) collective-permute-start(f32[8,128,64]{2,1,0:T(8,128)} %multiply_add_fusion.2), channel_id=1, source_target_pairs={{0,8},{8,16},{16,24},{24,32},{32,40},{40,48},{48,56},{56,64},{64,7... | collective-permute-start | bytes 786440 | tf_op jit(solution)/shard_map/while/body/eval_jaxpr/ppermute | solution.py:33
  323.0 15.4 %collective-permute-start = (f32[8,128,64]{2,1,0:T(8,128)}, f32[8,128,64]{2,1,0:T(8,128)S(1)}, u32[]{:S(2)}, u32[]{:S(2)}) collective-permute-start(f32[8,128,64]{2,1,0:T(8,128)} %multiply_add_fusion.2), channel_id=1, source_target_pairs={{0,8},{8,16},{16,24},{24,32},{32,40},{40,48},{48,56},{56,64},{64,7... | collective-permute-start | bytes 786440 | tf_op jit(solution)/shard_map/while/body/eval_jaxpr/ppermute | solution.py:33
  339.3 15.7 %collective-permute-start = (f32[8,128,64]{2,1,0:T(8,128)}, f32[8,128,64]{2,1,0:T(8,128)S(1)}, u32[]{:S(2)}, u32[]{:S(2)}) collective-permute-start(f32[8,128,64]{2,1,0:T(8,128)} %multiply_add_fusion.2), channel_id=1, source_target_pairs={{0,8},{8,16},{16,24},{24,32},{32,40},{40,48},{48,56},{56,64},{64,7... | collective-permute-start | bytes 786440 | tf_op jit(solution)/shard_map/while/body/eval_jaxpr/ppermute | solution.py:33
  355.9 14.3 %collective-permute-start = (f32[8,128,64]{2,1,0:T(8,128)}, f32[8,128,64]{2,1,0:T(8,128)S(1)}, u32[]{:S(2)}, u32[]{:S(2)}) collective-permute-start(f32[8,128,64]{2,1,0:T(8,128)} %multiply_add_fusion.2), channel_id=1, source_target_pairs={{0,8},{8,16},{16,24},{24,32},{32,40},{40,48},{48,56},{56,64},{64,7... | collective-permute-start | bytes 786440 | tf_op jit(solution)/shard_map/while/body/eval_jaxpr/ppermute | solution.py:33
  371.1 12.9 %collective-permute-start = (f32[8,128,64]{2,1,0:T(8,128)}, f32[8,128,64]{2,1,0:T(8,128)S(1)}, u32[]{:S(2)}, u32[]{:S(2)}) collective-permute-start(f32[8,128,64]{2,1,0:T(8,128)} %multiply_add_fusion.2), channel_id=1, source_target_pairs={{0,8},{8,16},{16,24},{24,32},{32,40},{40,48},{48,56},{56,64},{64,7... | collective-permute-start | bytes 786440 | tf_op jit(solution)/shard_map/while/body/eval_jaxpr/ppermute | solution.py:33
  384.9 13.0 %collective-permute-start = (f32[8,128,64]{2,1,0:T(8,128)}, f32[8,128,64]{2,1,0:T(8,128)S(1)}, u32[]{:S(2)}, u32[]{:S(2)}) collective-permute-start(f32[8,128,64]{2,1,0:T(8,128)} %multiply_add_fusion.2), channel_id=1, source_target_pairs={{0,8},{8,16},{16,24},{24,32},{32,40},{40,48},{48,56},{56,64},{64,7... | collective-permute-start | bytes 786440 | tf_op jit(solution)/shard_map/while/body/eval_jaxpr/ppermute | solution.py:33
  398.8 12.1 %collective-permute-start = (f32[8,128,64]{2,1,0:T(8,128)}, f32[8,128,64]{2,1,0:T(8,128)S(1)}, u32[]{:S(2)}, u32[]{:S(2)}) collective-permute-start(f32[8,128,64]{2,1,0:T(8,128)} %multiply_add_fusion.2), channel_id=1, source_target_pairs={{0,8},{8,16},{16,24},{24,32},{32,40},{40,48},{48,56},{56,64},{64,7... | collective-permute-start | bytes 786440 | tf_op jit(solution)/shard_map/while/body/eval_jaxpr/ppermute | solution.py:33
  411.8 11.6 %collective-permute-start = (f32[8,128,64]{2,1,0:T(8,128)}, f32[8,128,64]{2,1,0:T(8,128)S(1)}, u32[]{:S(2)}, u32[]{:S(2)}) collective-permute-start(f32[8,128,64]{2,1,0:T(8,128)} %multiply_add_fusion.2), channel_id=1, source_target_pairs={{0,8},{8,16},{16,24},{24,32},{32,40},{40,48},{48,56},{56,64},{64,7... | collective-permute-start | bytes 786440 | tf_op jit(solution)/shard_map/while/body/eval_jaxpr/ppermute | solution.py:33
  424.4 11.6 %collective-permute-start = (f32[8,128,64]{2,1,0:T(8,128)}, f32[8,128,64]{2,1,0:T(8,128)S(1)}, u32[]{:S(2)}, u32[]{:S(2)}) collective-permute-start(f32[8,128,64]{2,1,0:T(8,128)} %multiply_add_fusion.2), channel_id=1, source_target_pairs={{0,8},{8,16},{16,24},{24,32},{32,40},{40,48},{48,56},{56,64},{64,7... | collective-permute-start | bytes 786440 | tf_op jit(solution)/shard_map/while/body/eval_jaxpr/ppermute | solution.py:33
  449.4 12.4 %collective-permute-start = (f32[8,128,64]{2,1,0:T(8,128)}, f32[8,128,64]{2,1,0:T(8,128)S(1)}, u32[]{:S(2)}, u32[]{:S(2)}) collective-permute-start(f32[8,128,64]{2,1,0:T(8,128)} %multiply_add_fusion.2), channel_id=1, source_target_pairs={{0,8},{8,16},{16,24},{24,32},{32,40},{40,48},{48,56},{56,64},{64,7... | collective-permute-start | bytes 786440 | tf_op jit(solution)/shard_map/while/body/eval_jaxpr/ppermute | solution.py:33
  462.7 13.8 %collective-permute-start = (f32[8,128,64]{2,1,0:T(8,128)}, f32[8,128,64]{2,1,0:T(8,128)S(1)}, u32[]{:S(2)}, u32[]{:S(2)}) collective-permute-start(f32[8,128,64]{2,1,0:T(8,128)} %multiply_add_fusion.2), channel_id=1, source_target_pairs={{0,8},{8,16},{16,24},{24,32},{32,40},{40,48},{48,56},{56,64},{64,7... | collective-permute-start | bytes 786440 | tf_op jit(solution)/shard_map/while/body/eval_jaxpr/ppermute | solution.py:33
  477.4 15.3 %collective-permute-start = (f32[8,128,64]{2,1,0:T(8,128)}, f32[8,128,64]{2,1,0:T(8,128)S(1)}, u32[]{:S(2)}, u32[]{:S(2)}) collective-permute-start(f32[8,128,64]{2,1,0:T(8,128)} %multiply_add_fusion.2), channel_id=1, source_target_pairs={{0,8},{8,16},{16,24},{24,32},{32,40},{40,48},{48,56},{56,64},{64,7... | collective-permute-start | bytes 786440 | tf_op jit(solution)/shard_map/while/body/eval_jaxpr/ppermute | solution.py:33
  493.6 15.4 %collective-permute-start = (f32[8,128,64]{2,1,0:T(8,128)}, f32[8,128,64]{2,1,0:T(8,128)S(1)}, u32[]{:S(2)}, u32[]{:S(2)}) collective-permute-start(f32[8,128,64]{2,1,0:T(8,128)} %multiply_add_fusion.2), channel_id=1, source_target_pairs={{0,8},{8,16},{16,24},{24,32},{32,40},{40,48},{48,56},{56,64},{64,7... | collective-permute-start | bytes 786440 | tf_op jit(solution)/shard_map/while/body/eval_jaxpr/ppermute | solution.py:33
  509.9 16.5 %collective-permute-start = (f32[8,128,64]{2,1,0:T(8,128)}, f32[8,128,64]{2,1,0:T(8,128)S(1)}, u32[]{:S(2)}, u32[]{:S(2)}) collective-permute-start(f32[8,128,64]{2,1,0:T(8,128)} %multiply_add_fusion.2), channel_id=1, source_target_pairs={{0,8},{8,16},{16,24},{24,32},{32,40},{40,48},{48,56},{56,64},{64,7... | collective-permute-start | bytes 786440 | tf_op jit(solution)/shard_map/while/body/eval_jaxpr/ppermute | solution.py:33
  527.3 16.3 %collective-permute-start = (f32[8,128,64]{2,1,0:T(8,128)}, f32[8,128,64]{2,1,0:T(8,128)S(1)}, u32[]{:S(2)}, u32[]{:S(2)}) collective-permute-start(f32[8,128,64]{2,1,0:T(8,128)} %multiply_add_fusion.2), channel_id=1, source_target_pairs={{0,8},{8,16},{16,24},{24,32},{32,40},{40,48},{48,56},{56,64},{64,7... | collective-permute-start | bytes 786440 | tf_op jit(solution)/shard_map/while/body/eval_jaxpr/ppermute | solution.py:33
  544.5 19.2 %collective-permute-start = (f32[8,128,64]{2,1,0:T(8,128)}, f32[8,128,64]{2,1,0:T(8,128)S(1)}, u32[]{:S(2)}, u32[]{:S(2)}) collective-permute-start(f32[8,128,64]{2,1,0:T(8,128)} %multiply_add_fusion.2), channel_id=1, source_target_pairs={{0,8},{8,16},{16,24},{24,32},{32,40},{40,48},{48,56},{56,64},{64,7... | collective-permute-start | bytes 786440 | tf_op jit(solution)/shard_map/while/body/eval_jaxpr/ppermute | solution.py:33
  564.6 17.1 %collective-permute-start = (f32[8,128,64]{2,1,0:T(8,128)}, f32[8,128,64]{2,1,0:T(8,128)S(1)}, u32[]{:S(2)}, u32[]{:S(2)}) collective-permute-start(f32[8,128,64]{2,1,0:T(8,128)} %multiply_add_fusion.2), channel_id=1, source_target_pairs={{0,8},{8,16},{16,24},{24,32},{32,40},{40,48},{48,56},{56,64},{64,7... | collective-permute-start | bytes 786440 | tf_op jit(solution)/shard_map/while/body/eval_jaxpr/ppermute | solution.py:33
  582.5 15.1 %collective-permute-start = (f32[8,128,64]{2,1,0:T(8,128)}, f32[8,128,64]{2,1,0:T(8,128)S(1)}, u32[]{:S(2)}, u32[]{:S(2)}) collective-permute-start(f32[8,128,64]{2,1,0:T(8,128)} %multiply_add_fusion.2), channel_id=1, source_target_pairs={{0,8},{8,16},{16,24},{24,32},{32,40},{40,48},{48,56},{56,64},{64,7... | collective-permute-start | bytes 786440 | tf_op jit(solution)/shard_map/while/body/eval_jaxpr/ppermute | solution.py:33
  598.5 13.4 %collective-permute-start = (f32[8,128,64]{2,1,0:T(8,128)}, f32[8,128,64]{2,1,0:T(8,128)S(1)}, u32[]{:S(2)}, u32[]{:S(2)}) collective-permute-start(f32[8,128,64]{2,1,0:T(8,128)} %multiply_add_fusion.2), channel_id=1, source_target_pairs={{0,8},{8,16},{16,24},{24,32},{32,40},{40,48},{48,56},{56,64},{64,7... | collective-permute-start | bytes 786440 | tf_op jit(solution)/shard_map/while/body/eval_jaxpr/ppermute | solution.py:33
  649.4 12.5 %collective-permute-start = (f32[8,128,64]{2,1,0:T(8,128)}, f32[8,128,64]{2,1,0:T(8,128)S(1)}, u32[]{:S(2)}, u32[]{:S(2)}) collective-permute-start(f32[8,128,64]{2,1,0:T(8,128)} %multiply_add_fusion.2), channel_id=1, source_target_pairs={{0,8},{8,16},{16,24},{24,32},{32,40},{40,48},{48,56},{56,64},{64,7... | collective-permute-start | bytes 786440 | tf_op jit(solution)/shard_map/while/body/eval_jaxpr/ppermute | solution.py:33
  (35 other events, 931.3 us)
Sparse Core Ops, SparseCore 0:
  9.9 75.1 all-gather.6
  87.7 80.6 all-gather.4
  171.0 75.2 all-gather.8
  755.6 74.5 reduce-scatter.1
